TPU v7x, 32 devices: a whole 2x2x4 slice. The times are simulated.
32 devices in a mesh: ep: 16 (over z, y, core), dp: 2 (over x).
Axes of the slice: x: 2, y: 2, z: 4, core: 2. Of those that a mesh axis runs over, the one named last changes fastest.
Arguments:
- moe_rows: bfloat16 [1024, 3584], P(('dp', 'ep')), parts along dimension 0, may hold values from -6 to 6
- routes: int32 [1024, 4], P(('dp', 'ep')), parts along dimension 0, may hold values from 0 to 7, all different within a row; in each aligned block of 32 rows (0 to 31, 32 to 63, ...) at most 32 rows name the same one
- route_weights: float32 [1024, 4], P(('dp', 'ep')), parts along dimension 0, may hold values from 0.05 to 0.5
- w_gate: bfloat16 [16, 3584, 512], P('ep'), may hold values from -0.09375 to 0.09375
- w_up: bfloat16 [16, 3584, 512], P('ep'), may hold values from -0.09375 to 0.09375
- w_down: bfloat16 [16, 512, 3584], P('ep'), may hold values from -0.1875 to 0.1875
- queries: bfloat16 [128, 64, 576], P(('dp', 'ep')), parts along dimension 0, may hold values from -45 to 45
- latent_cache: bfloat16 [128, 128, 576], P(('dp', 'ep')), parts along dimension 0, may hold values from -6 to 6
- lengths: int32 [128], P(('dp', 'ep')), parts along dimension 0, may hold values from 2 to 128, as said below
Outputs:
- moe_out: bfloat16 [1024, 3584], P(('dp', 'ep')), parts along dimension 0
- attn_out: bfloat16 [128, 64, 512], P(('dp', 'ep')), parts along dimension 0
There are 2 independent parts, one for each index of `dp`. A program takes and returns all parts, laid end to end along the dimension named above; an argument that names none is the same for every part. Nothing has to cross between parts.
Inputs may be any that keep to these rules, and one draw needn't show every extreme that they name: `routes`: each row names 4 different experts; in each aligned block of 32 rows (the rows of one device) no expert is named by more than 32 rows, a bound that some block reaches. `lengths`: some row of every part uses all 128 positions.
All inputs are finite; a program needn't handle non-finite values.
Results may differ from a plain program's by a relative error of at most 0.0085.
Values may be sent and summed in bfloat16 or wider, within the bound.
No kernel may reach another device: no remote copies, remote signals or barrier semaphores. Data moves between devices by JAX's collectives and lax.ppermute only.
A program may use at most 128 MiB of HBM per device.

v0:
```python
import jax
import jax.numpy as jnp
from jax import lax
from jax.sharding import PartitionSpec as P

LATENT = 512
score_scale = 192.0 ** (-0.5)


def attend(queries, latent_cache, lengths):
    scores = (
        jnp.einsum("rhc,rlc->rhl", queries, latent_cache, preferred_element_type=jnp.float32)
        * score_scale
    )
    in_range = (
        jnp.arange(latent_cache.shape[1], dtype=jnp.int32)[None, None, :] < lengths[:, None, None]
    )
    scores = jnp.where(in_range, scores, -1e30)
    highest = jnp.max(scores, axis=-1, keepdims=True)
    expo = jnp.where(in_range, jnp.exp(scores - highest), 0.0)
    probs = (expo / jnp.sum(expo, axis=-1, keepdims=True)).astype(jnp.bfloat16)
    return jnp.einsum(
        "rhl,rlc->rhc", probs, latent_cache[:, :, :LATENT], preferred_element_type=jnp.float32
    ).astype(jnp.bfloat16)


def shards(moe_rows, routes, route_weights, w_gate, w_up, w_down, queries, latent_cache, lengths):
    attn_out = attend(queries, latent_cache, lengths)
    rows_here, model_width = moe_rows.shape
    experts = lax.axis_size("ep") // 2
    expert = lax.axis_index("ep") // 2
    named = routes[:, :, None] == jnp.arange(experts, dtype=jnp.int32)[None, None, :]
    dense_w = jnp.sum(jnp.where(named, route_weights[:, :, None], 0.0), axis=1)
    hi = dense_w.astype(jnp.bfloat16)
    rest = dense_w - hi.astype(jnp.float32)
    mid = rest.astype(jnp.bfloat16)
    lo = (rest - mid.astype(jnp.float32)).astype(jnp.bfloat16)
    extra = -(-3 * experts // 128) * 128
    tail = jnp.zeros((rows_here, extra - 3 * experts), jnp.bfloat16)
    packed = jnp.concatenate([moe_rows, hi, mid, lo, tail], axis=1)
    gathered = lax.all_gather(packed, "ep", axis=0, tiled=True)
    all_rows = gathered[:, :model_width]
    parts = gathered[:, model_width : model_width + 3 * experts].astype(jnp.float32)
    parts = parts.reshape(-1, 3, experts)
    weight_all = parts[:, 0] + (parts[:, 1] + parts[:, 2])
    weight = jnp.sum(jnp.where(jnp.arange(experts)[None, :] == expert, weight_all, 0.0), axis=1)
    gate_act = jnp.dot(all_rows, w_gate[0], preferred_element_type=jnp.float32)
    up_act = jnp.dot(all_rows, w_up[0], preferred_element_type=jnp.float32)
    hidden = (jax.nn.silu(gate_act) * up_act).astype(jnp.bfloat16)
    partial_out = jnp.dot(hidden, w_down[0], preferred_element_type=jnp.float32)
    partial_out = partial_out * weight[:, None]
    moe_out = lax.psum_scatter(partial_out, "ep", scatter_dimension=0, tiled=True)
    return (moe_out.astype(jnp.bfloat16), attn_out)


def solution(mesh):
    in_specs = (
        P(("dp", "ep"), None),
        P(("dp", "ep"), None),
        P(("dp", "ep"), None),
        P("ep", None, None),
        P("ep", None, None),
        P("ep", None, None),
        P(("dp", "ep"), None, None),
        P(("dp", "ep"), None, None),
        P(("dp", "ep")),
    )
    out_specs = (P(("dp", "ep"), None), P(("dp", "ep"), None, None))
    return jax.shard_map(shards, mesh=mesh, in_specs=in_specs, out_specs=out_specs, check_vma=False)
```

profile of v0, /device:TPU:0, one launch (start us, length us, event | category | flops | bytes accessed | tf_op | source)
XLA Modules:
  0.0 178.8 jit_solution(15685329627394911693)
XLA Ops:
  7.2 0.0 copy-start
  7.2 0.0 all-gather.2.cloned.1.call-start
  7.2 0.7 select_reduce_fusion
  8.0 0.1 copy.22
  8.1 0.1 copy.23
  8.2 0.1 copy.24
  8.3 1.7 concatenate.3
  10.0 0.0 all-gather.2.cloned.1.call-update
  10.0 0.0 reduce-scatter.2.cloned.1.call-start
  10.1 51.7 %all-gather.2.cloned.1.call-done = bf16[512,3712]{1,0:T(8,128)(2,1)} async-done(((bf16[32,3712]{1,0:T(8,128)(2,1)}), bf16[512,3712]{1,0:T(8,128)(2,1)}) %all-gather.2.cloned.1.call-update) | async-done | bytes 3801104 | tf_op jit(solution)/shard_map/all_gather | solution.py:41
  61.7 0.9 slice.25
  62.6 0.1 copy.27
  62.7 0.1 fusion.32
  62.8 5.2 %fusion.4 = f32[512,512]{1,0:T(8,128)S(1)} fusion(bf16[1,3584,512]{2,1,0:T(8,128)(2,1)} %param.12, bf16[512,3712]{1,0:T(8,128)(2,1)} %all-gather.2.cloned.1.call-done), kind=kOutput, calls=%fused_computation.5 | convolution fusion | flops 1879048192 | bytes 8388608 | tf_op jit(solution)/shard_map/dot_general | solution.py:47
  68.0 11.2 %convolution_multiply_fusion = f32[512,3584]{1,0:T(8,128)} fusion(bf16[1,512,3584]{2,1,0:T(8,128)(2,1)} %param.14, f32[512]{0:T(512)S(1)} %fusion.32, bf16[1,3584,512]{2,1,0:T(8,128)(2,1)} %param.13, bf16[512,3712]{1,0:T(8,128)(2,1)} %all-gather.2.cloned.1.call-done, f32[512,512]{1,0:T(8,128)S(1)} %fusion.4), kind=kOutput, calls=%fused_computation.1 | convolution fusion | flops 3761504256 | bytes 19400704 | tf_op jit(solution)/shard_map/dot_general | solution.py:50
  79.3 0.0 copy-start.2
  79.3 0.0 copy-start.1
  79.3 0.0 reduce-scatter.2.cloned.1.call-update
  79.3 0.6 copy-done.2
  79.9 0.1 iota_compare_fusion.1
  80.0 0.0 copy-done
  80.0 0.3 copy-done.1
  80.3 0.2 fusion.19
  80.6 0.2 fusion.37
  80.8 1.3 convolution_convert_fusion
  82.1 88.2 %reduce-scatter.2.cloned.1.call-done = f32[32,3584]{1,0:T(8,128)} async-done(((f32[512,3584]{1,0:T(8,128)}), f32[32,3584]{1,0:T(8,128)}) %reduce-scatter.2.cloned.1.call-update) | async-done | bytes 458768 | tf_op jit(solution)/shard_map/reduce_scatter | solution.py:52
  170.2 1.7 convert_element_type.34
  (4 shorter events, 0.0 us)
Async XLA Ops:
  7.2 72.8 %copy-start = (bf16[4,64,576]{2,1,0:T(8,128)(2,1)S(1)}, bf16[4,64,576]{2,1,0:T(8,128)(2,1)}, u32[]{:S(2)}) copy-start(bf16[4,64,576]{2,1,0:T(8,128)(2,1)} %param.15) | copy-start | bytes 884740
  7.2 54.6 %all-gather.2.cloned.1.call-start = ((), (), s32[]{:S(2)}) async-start(), calls=%async_computation.1 | async-start | bytes 4038656 | tf_op jit(solution)/shard_map/all_gather | solution.py:41
  10.0 160.2 %reduce-scatter.2.cloned.1.call-start = ((), (), s32[]{:S(2)}) async-start(), calls=%async_computation.2 | async-start | bytes 7798784 | tf_op jit(solution)/shard_map/reduce_scatter | solution.py:52
  79.3 0.7 copy-start.2
  79.3 1.1 copy-start.1
Sparse Core Ops, SparseCore 0:
  10.9 50.8 all-gather.1
  79.4 90.7 reduce-scatter.1
where the time goes:
time: 179 us
  waiting for transfers between devices  140 us (78%)
  matrix products  18 us (10%)
  between operations  14.1 us (8%)
  local copies, waits for them, and re-layouts  3.97 us (2%)
  other arithmetic  2.85 us (2%)
    reduce_scatter x1, waiting for transfers between devices, shards(): lax.psum_scatter(partial_out, 'ep', scatter_dimension=0, tiled=True)  88.2 us
    all_gather x1, waiting for transfers between devices, shards(): gathered = lax.all_gather(packed, 'ep', axis=0, tiled=True)  51.7 us
    dot_general x1, matrix products, shards(): partial_out = jnp.dot(hidden, w_down[0], preferred_element_type=jnp.float32)  11.2 us
    dot_general x1, matrix products, shards(): gate_act = jnp.dot(all_rows, w_gate[0], preferred_element_type=jnp.float32)  5.21 us
  transfers between devices with their start and end apart: 2, of which 2 were waited for; matrix products, arithmetic and copies ran while one was open for 1% of the time, Pallas kernels for 0%

commit v1 on v0

--- a/solution.py
+++ b/solution.py
@@ -38,7 +38,13 @@
     extra = -(-3 * experts // 128) * 128
     tail = jnp.zeros((rows_here, extra - 3 * experts), jnp.bfloat16)
     packed = jnp.concatenate([moe_rows, hi, mid, lo, tail], axis=1)
-    gathered = lax.all_gather(packed, "ep", axis=0, tiled=True)
+    size = lax.axis_size("ep")
+    moving, blocks = (packed, [packed])
+    for _ in range(size - 1):
+        moving = lax.ppermute(moving, "ep", [(i, (i + 1) % size) for i in range(size)])
+        blocks.insert(0, moving)
+    flat = jnp.concatenate(blocks, axis=0)
+    gathered = jnp.roll(flat, (lax.axis_index("ep") + 1) * packed.shape[0], axis=0)
     all_rows = gathered[:, :model_width]
     parts = gathered[:, model_width : model_width + 3 * experts].astype(jnp.float32)
     parts = parts.reshape(-1, 3, experts)

time: 179 us -> 320 us (1.79); the launches traced: 179 us -> 316 us
  local copies, waits for them, and re-layouts: 3.97 us -> 70.4 us
  waiting for transfers between devices: 140 us -> 206 us
    ppermute x0 -> x15, waiting for transfers between devices: none -> 116 us  [shards(): lax.ppermute(moving, 'ep', [(i, (i + 1) % size) for i in range(size)])]
    all_gather x1 -> x0, waiting for transfers between devices: 51.7 us -> none  [shards(): gathered = lax.all_gather(packed, 'ep', axis=0, tiled=True)]
    concatenate x0 -> x1, local copies, waits for them, and re-layouts: none -> 33.6 us  [shards(): jnp.roll(flat, (lax.axis_index('ep') + 1) * packed.shape[0], axis=0)]
    ppermute x0 -> x15, local copies, waits for them, and re-layouts: none -> 28.3 us  [shards(): lax.ppermute(moving, 'ep', [(i, (i + 1) % size) for i in range(size)])]
    unnamed x7 -> x34, local copies, waits for them, and re-layouts: 1.07 us -> 8.02 us
  transfers between devices with their start and end apart: 2 -> 16, of which waited for: 2 -> 15; matrix products, arithmetic and copies ran while one was open for 1% -> 9% of each run, Pallas kernels for 0% -> 0%
where the time goes in v1:
time: 320 us; the launch traced here: 316 us
  waiting for transfers between devices  206 us (64%)
  local copies, waits for them, and re-layouts  70.4 us (22%)
  matrix products  20.9 us (7%)
  between operations  14.1 us (4%)
  other arithmetic  3.68 us (1%)
    ppermute x15, waiting for transfers between devices, shards(): lax.ppermute(moving, 'ep', [(i, (i + 1) % size) for i in range(size)])  116 us
    reduce_scatter x1, waiting for transfers between devices, shards(): lax.psum_scatter(partial_out, 'ep', scatter_dimension=0, tiled=True)  90.1 us
    concatenate x1, local copies, waits for them, and re-layouts, shards(): jnp.roll(flat, (lax.axis_index('ep') + 1) * packed.shape[0], axis=0)  33.6 us
    ppermute x15, local copies, waits for them, and re-layouts, shards(): lax.ppermute(moving, 'ep', [(i, (i + 1) % size) for i in range(size)])  28.3 us
    dot_general x1, matrix products, shards(): partial_out = jnp.dot(hidden, w_down[0], preferred_element_type=jnp.float32)  13.2 us
    unnamed x34, local copies, waits for them, and re-layouts  8.02 us
  transfers between devices with their start and end apart: 16, of which 15 were waited for; matrix products, arithmetic and copies ran while one was open for 9% of the time, Pallas kernels for 0%

profile of v1, /device:TPU:0, one launch (start us, length us, event | category | flops | bytes accessed | tf_op | source)
XLA Modules:
  0.0 315.6 jit_solution(5471722091449369583)
XLA Ops:
  7.2 1.4 copy.89
  8.7 0.7 select_reduce_fusion
  9.8 0.5 collective-permute-start
  10.3 8.8 %collective-permute-done = bf16[32,3712]{1,0:T(8,128)(2,1)S(1)} collective-permute-done((bf16[32,3712]{1,0:T(8,128)(2,1)S(1)}, bf16[32,3712]{1,0:T(8,128)(2,1)S(1)}, u32[]{:S(2)}, u32[]{:S(2)}) %collective-permute-start) | collective-permute-done | bytes 237600 | tf_op jit(solution)/shard_map/ppermute | solution.py:44
  19.1 8.2 %collective-permute-done.1 = bf16[32,3712]{1,0:T(8,128)(2,1)S(1)} collective-permute-done((bf16[32,3712]{1,0:T(8,128)(2,1)S(1)}, bf16[32,3712]{1,0:T(8,128)(2,1)S(1)}, u32[]{:S(2)}, u32[]{:S(2)}) %collective-permute-start.1) | collective-permute-done | bytes 237600 | tf_op jit(solution)/shard_map/ppermute | solution.py:44
  27.3 8.2 %collective-permute-done.2 = bf16[32,3712]{1,0:T(8,128)(2,1)S(1)} collective-permute-done((bf16[32,3712]{1,0:T(8,128)(2,1)S(1)}, bf16[32,3712]{1,0:T(8,128)(2,1)S(1)}, u32[]{:S(2)}, u32[]{:S(2)}) %collective-permute-start.2) | collective-permute-done | bytes 237600 | tf_op jit(solution)/shard_map/ppermute | solution.py:44
  35.6 8.2 %collective-permute-done.3 = bf16[32,3712]{1,0:T(8,128)(2,1)S(1)} collective-permute-done((bf16[32,3712]{1,0:T(8,128)(2,1)S(1)}, bf16[32,3712]{1,0:T(8,128)(2,1)S(1)}, u32[]{:S(2)}, u32[]{:S(2)}) %collective-permute-start.3) | collective-permute-done | bytes 237600 | tf_op jit(solution)/shard_map/ppermute | solution.py:44
  43.8 8.2 %collective-permute-done.4 = bf16[32,3712]{1,0:T(8,128)(2,1)S(1)} collective-permute-done((bf16[32,3712]{1,0:T(8,128)(2,1)S(1)}, bf16[32,3712]{1,0:T(8,128)(2,1)S(1)}, u32[]{:S(2)}, u32[]{:S(2)}) %collective-permute-start.4) | collective-permute-done | bytes 237600 | tf_op jit(solution)/shard_map/ppermute | solution.py:44
  52.0 8.2 %collective-permute-done.5 = bf16[32,3712]{1,0:T(8,128)(2,1)S(1)} collective-permute-done((bf16[32,3712]{1,0:T(8,128)(2,1)S(1)}, bf16[32,3712]{1,0:T(8,128)(2,1)S(1)}, u32[]{:S(2)}, u32[]{:S(2)}) %collective-permute-start.5) | collective-permute-done | bytes 237600 | tf_op jit(solution)/shard_map/ppermute | solution.py:44
  60.3 0.7 copy-done.5
  61.0 8.2 %collective-permute-done.6 = bf16[32,3712]{1,0:T(8,128)(2,1)S(1)} collective-permute-done((bf16[32,3712]{1,0:T(8,128)(2,1)S(1)}, bf16[32,3712]{1,0:T(8,128)(2,1)S(1)}, u32[]{:S(2)}, u32[]{:S(2)}) %collective-permute-start.6) | collective-permute-done | bytes 237600 | tf_op jit(solution)/shard_map/ppermute | solution.py:44
  69.2 0.7 copy-done.7
  69.9 8.2 %collective-permute-done.7 = bf16[32,3712]{1,0:T(8,128)(2,1)S(1)} collective-permute-done((bf16[32,3712]{1,0:T(8,128)(2,1)S(1)}, bf16[32,3712]{1,0:T(8,128)(2,1)S(1)}, u32[]{:S(2)}, u32[]{:S(2)}) %collective-permute-start.7) | collective-permute-done | bytes 237600 | tf_op jit(solution)/shard_map/ppermute | solution.py:44
  78.1 0.7 copy-done.8
  78.8 8.2 %collective-permute-done.8 = bf16[32,3712]{1,0:T(8,128)(2,1)S(1)} collective-permute-done((bf16[32,3712]{1,0:T(8,128)(2,1)S(1)}, bf16[32,3712]{1,0:T(8,128)(2,1)S(1)}, u32[]{:S(2)}, u32[]{:S(2)}) %collective-permute-start.8) | collective-permute-done | bytes 237600 | tf_op jit(solution)/shard_map/ppermute | solution.py:44
  87.0 0.7 copy-done.9
  87.7 8.2 %collective-permute-done.9 = bf16[32,3712]{1,0:T(8,128)(2,1)S(1)} collective-permute-done((bf16[32,3712]{1,0:T(8,128)(2,1)S(1)}, bf16[32,3712]{1,0:T(8,128)(2,1)S(1)}, u32[]{:S(2)}, u32[]{:S(2)}) %collective-permute-start.9) | collective-permute-done | bytes 237600 | tf_op jit(solution)/shard_map/ppermute | solution.py:44
  96.0 0.7 copy-done.10
  96.7 8.2 %collective-permute-done.10 = bf16[32,3712]{1,0:T(8,128)(2,1)S(1)} collective-permute-done((bf16[32,3712]{1,0:T(8,128)(2,1)S(1)}, bf16[32,3712]{1,0:T(8,128)(2,1)S(1)}, u32[]{:S(2)}, u32[]{:S(2)}) %collective-permute-start.10) | collective-permute-done | bytes 237600 | tf_op jit(solution)/shard_map/ppermute | solution.py:44
  104.9 0.7 copy-done.12
  105.6 8.2 %collective-permute-done.11 = bf16[32,3712]{1,0:T(8,128)(2,1)S(1)} collective-permute-done((bf16[32,3712]{1,0:T(8,128)(2,1)S(1)}, bf16[32,3712]{1,0:T(8,128)(2,1)S(1)}, u32[]{:S(2)}, u32[]{:S(2)}) %collective-permute-start.11) | collective-permute-done | bytes 237600 | tf_op jit(solution)/shard_map/ppermute | solution.py:44
  113.8 0.7 copy-done.13
  114.5 8.2 %collective-permute-done.12 = bf16[32,3712]{1,0:T(8,128)(2,1)S(1)} collective-permute-done((bf16[32,3712]{1,0:T(8,128)(2,1)S(1)}, bf16[32,3712]{1,0:T(8,128)(2,1)S(1)}, u32[]{:S(2)}, u32[]{:S(2)}) %collective-permute-start.12) | collective-permute-done | bytes 237600 | tf_op jit(solution)/shard_map/ppermute | solution.py:44
  122.7 0.7 copy-done.14
  123.4 8.3 %collective-permute-done.13 = bf16[32,3712]{1,0:T(8,128)(2,1)} collective-permute-done((bf16[32,3712]{1,0:T(8,128)(2,1)S(1)}, bf16[32,3712]{1,0:T(8,128)(2,1)}, u32[]{:S(2)}, u32[]{:S(2)}) %collective-permute-start.13) | collective-permute-done | bytes 237600 | tf_op jit(solution)/shard_map/ppermute | solution.py:44
  131.8 0.5 copy.105
  132.3 0.5 copy.104
  132.7 2.4 copy.103
  135.1 2.3 copy.102
  137.4 2.2 copy.101
  139.6 1.3 copy.100
  140.9 2.3 copy.99
  143.2 2.3 copy.98
  145.5 2.2 copy.97
  147.7 1.3 copy.96
  149.0 2.2 copy.95
  151.3 2.2 copy.94
  153.5 2.2 copy.93
  155.7 2.2 copy.92
  158.0 2.2 copy.91
  160.2 33.6 %concatenate.10 = bf16[1024,3712]{0,1:T(8,128)(2,1)} concatenate(bf16[32,3712]{0,1:T(8,128)(2,1)} %copy.91, bf16[32,3712]{0,1:T(8,128)(2,1)} %copy.92, bf16[32,3712]{0,1:T(8,128)(2,1)} %copy.93, bf16[32,3712]{0,1:T(8,128)(2,1)} %copy.94, bf16[32,3712]{0,1:T(8,128)(2,1)} %copy.95, bf16[32,3712]{0,1:T(8,128)(2,1)} %copy.96, bf16[32,3712]{0,1:T(8,128)(2,1)} %copy.97, ...), dimensions={0} | concatenate | bytes 15204352 | tf_op jit(solution)/shard_map/jit(_roll_dynamic)/concatenate | solution.py:47
  193.8 6.1 %fusion.2 = f32[512,512]{1,0:T(8,128)S(1)} fusion(bf16[1,3584,512]{2,1,0:T(8,128)(2,1)} %param.13, bf16[1024,3712]{0,1:T(8,128)(2,1)} %concatenate.10, s32[]{:T(128)S(6)} %select_n.34), kind=kOutput, calls=%fused_computation.3 | convolution fusion | flops 1879048192 | bytes 8388612 | tf_op jit(solution)/shard_map/dot_general | solution.py:54
  200.0 0.8 fusion.15
  200.9 13.2 %convolution_multiply_fusion = f32[512,3584]{1,0:T(8,128)} fusion(bf16[1,512,3584]{2,1,0:T(8,128)(2,1)} %param.14, f32[512]{0:T(512)S(1)} %fusion.19, f32[512,512]{1,0:T(8,128)S(1)} %fusion.2, bf16[1,3584,512]{2,1,0:T(8,128)(2,1)} %param.12, bf16[1024,3712]{0,1:T(8,128)(2,1)} %concatenate.10, s32[]{:T(128)S(6)} %select_n.34), kind=kOutput, calls=%fused_computation.1 | convolution fusion | flops 3761504256 | bytes 19400708 | tf_op jit(solution)/shard_map/dot_general | solution.py:56
  214.2 0.6 copy-done.15
  215.7 1.3 convolution_convert_fusion
  217.0 90.1 %reduce-scatter.2.cloned.1.call-done = f32[32,3584]{1,0:T(8,128)} async-done(((f32[512,3584]{1,0:T(8,128)}), f32[32,3584]{1,0:T(8,128)}) %reduce-scatter.2.cloned.1.call-update) | async-done | bytes 458768 | tf_op jit(solution)/shard_map/reduce_scatter | solution.py:58
  307.1 1.7 convert_element_type.34
  (51 shorter events, 1.5 us)
Async XLA Ops:
  7.2 207.7 %copy-start = (bf16[4,64,576]{2,1,0:T(8,128)(2,1)S(1)}, bf16[4,64,576]{2,1,0:T(8,128)(2,1)}, u32[]{:S(2)}) copy-start(bf16[4,64,576]{2,1,0:T(8,128)(2,1)} %param.15) | copy-start | bytes 884740
  7.2 299.9 %reduce-scatter.2.cloned.1.call-start = ((), (), s32[]{:S(2)}) async-start(), calls=%async_computation.1 | async-start | bytes 7798784 | tf_op jit(solution)/shard_map/reduce_scatter | solution.py:58
  9.8 9.3 %collective-permute-start = (bf16[32,3712]{1,0:T(8,128)(2,1)S(1)}, bf16[32,3712]{1,0:T(8,128)(2,1)S(1)}, u32[]{:S(2)}, u32[]{:S(2)}) collective-permute-start(bf16[32,3712]{1,0:T(8,128)(2,1)S(1)} %copy.90), channel_id=1, source_target_pairs={{0,2},{2,4},{4,6},{6,8},{8,10},{10,12},{12,14},{14,16},{16,18},{18... | collective-permute-start | bytes 712712 | tf_op jit(solution)/shard_map/ppermute | solution.py:44
  19.1 8.2 %collective-permute-start.1 = (bf16[32,3712]{1,0:T(8,128)(2,1)S(1)}, bf16[32,3712]{1,0:T(8,128)(2,1)S(1)}, u32[]{:S(2)}, u32[]{:S(2)}) collective-permute-start(bf16[32,3712]{1,0:T(8,128)(2,1)S(1)} %collective-permute-done), channel_id=1, source_target_pairs={{0,2},{2,4},{4,6},{6,8},{8,10},{10,12},{12,14},{14,16},{16,18},{18... | collective-permute-start | bytes 712712 | tf_op jit(solution)/shard_map/ppermute | solution.py:44
  27.3 8.2 %collective-permute-start.2 = (bf16[32,3712]{1,0:T(8,128)(2,1)S(1)}, bf16[32,3712]{1,0:T(8,128)(2,1)S(1)}, u32[]{:S(2)}, u32[]{:S(2)}) collective-permute-start(bf16[32,3712]{1,0:T(8,128)(2,1)S(1)} %collective-permute-done.1), channel_id=1, source_target_pairs={{0,2},{2,4},{4,6},{6,8},{8,10},{10,12},{12,14},{14,16},{16,18},{18... | collective-permute-start | bytes 712712 | tf_op jit(solution)/shard_map/ppermute | solution.py:44
  35.6 96.2 %copy-start.2 = (bf16[32,3712]{1,0:T(8,128)(2,1)}, bf16[32,3712]{1,0:T(8,128)(2,1)S(1)}, u32[]{:S(2)}) copy-start(bf16[32,3712]{1,0:T(8,128)(2,1)S(1)} %collective-permute-done.2) | copy-start | bytes 712708
  35.6 8.2 %collective-permute-start.3 = (bf16[32,3712]{1,0:T(8,128)(2,1)S(1)}, bf16[32,3712]{1,0:T(8,128)(2,1)S(1)}, u32[]{:S(2)}, u32[]{:S(2)}) collective-permute-start(bf16[32,3712]{1,0:T(8,128)(2,1)S(1)} %collective-permute-done.2), channel_id=1, source_target_pairs={{0,2},{2,4},{4,6},{6,8},{8,10},{10,12},{12,14},{14,16},{16,18},{18... | collective-permute-start | bytes 712712 | tf_op jit(solution)/shard_map/ppermute | solution.py:44
  43.8 88.0 %copy-start.3 = (bf16[32,3712]{1,0:T(8,128)(2,1)}, bf16[32,3712]{1,0:T(8,128)(2,1)S(1)}, u32[]{:S(2)}) copy-start(bf16[32,3712]{1,0:T(8,128)(2,1)S(1)} %collective-permute-done.3) | copy-start | bytes 712708
  43.8 8.2 %collective-permute-start.4 = (bf16[32,3712]{1,0:T(8,128)(2,1)S(1)}, bf16[32,3712]{1,0:T(8,128)(2,1)S(1)}, u32[]{:S(2)}, u32[]{:S(2)}) collective-permute-start(bf16[32,3712]{1,0:T(8,128)(2,1)S(1)} %collective-permute-done.3), channel_id=1, source_target_pairs={{0,2},{2,4},{4,6},{6,8},{8,10},{10,12},{12,14},{14,16},{16,18},{18... | collective-permute-start | bytes 712712 | tf_op jit(solution)/shard_map/ppermute | solution.py:44
  52.0 79.8 %copy-start.4 = (bf16[32,3712]{1,0:T(8,128)(2,1)}, bf16[32,3712]{1,0:T(8,128)(2,1)S(1)}, u32[]{:S(2)}) copy-start(bf16[32,3712]{1,0:T(8,128)(2,1)S(1)} %collective-permute-done.4) | copy-start | bytes 712708
  52.0 8.2 %collective-permute-start.5 = (bf16[32,3712]{1,0:T(8,128)(2,1)S(1)}, bf16[32,3712]{1,0:T(8,128)(2,1)S(1)}, u32[]{:S(2)}, u32[]{:S(2)}) collective-permute-start(bf16[32,3712]{1,0:T(8,128)(2,1)S(1)} %collective-permute-done.4), channel_id=1, source_target_pairs={{0,2},{2,4},{4,6},{6,8},{8,10},{10,12},{12,14},{14,16},{16,18},{18... | collective-permute-start | bytes 712712 | tf_op jit(solution)/shard_map/ppermute | solution.py:44
  60.3 0.7 copy-start.5
  61.0 8.2 %collective-permute-start.6 = (bf16[32,3712]{1,0:T(8,128)(2,1)S(1)}, bf16[32,3712]{1,0:T(8,128)(2,1)S(1)}, u32[]{:S(2)}, u32[]{:S(2)}) collective-permute-start(bf16[32,3712]{1,0:T(8,128)(2,1)S(1)} %collective-permute-done.5), channel_id=1, source_target_pairs={{0,2},{2,4},{4,6},{6,8},{8,10},{10,12},{12,14},{14,16},{16,18},{18... | collective-permute-start | bytes 712712 | tf_op jit(solution)/shard_map/ppermute | solution.py:44
  69.2 0.7 copy-start.7
  69.9 8.2 %collective-permute-start.7 = (bf16[32,3712]{1,0:T(8,128)(2,1)S(1)}, bf16[32,3712]{1,0:T(8,128)(2,1)S(1)}, u32[]{:S(2)}, u32[]{:S(2)}) collective-permute-start(bf16[32,3712]{1,0:T(8,128)(2,1)S(1)} %collective-permute-done.6), channel_id=1, source_target_pairs={{0,2},{2,4},{4,6},{6,8},{8,10},{10,12},{12,14},{14,16},{16,18},{18... | collective-permute-start | bytes 712712 | tf_op jit(solution)/shard_map/ppermute | solution.py:44
  78.1 0.7 copy-start.8
  78.8 8.2 %collective-permute-start.8 = (bf16[32,3712]{1,0:T(8,128)(2,1)S(1)}, bf16[32,3712]{1,0:T(8,128)(2,1)S(1)}, u32[]{:S(2)}, u32[]{:S(2)}) collective-permute-start(bf16[32,3712]{1,0:T(8,128)(2,1)S(1)} %collective-permute-done.7), channel_id=1, source_target_pairs={{0,2},{2,4},{4,6},{6,8},{8,10},{10,12},{12,14},{14,16},{16,18},{18... | collective-permute-start | bytes 712712 | tf_op jit(solution)/shard_map/ppermute | solution.py:44
  87.0 0.7 copy-start.9
  87.7 8.2 %collective-permute-start.9 = (bf16[32,3712]{1,0:T(8,128)(2,1)S(1)}, bf16[32,3712]{1,0:T(8,128)(2,1)S(1)}, u32[]{:S(2)}, u32[]{:S(2)}) collective-permute-start(bf16[32,3712]{1,0:T(8,128)(2,1)S(1)} %collective-permute-done.8), channel_id=1, source_target_pairs={{0,2},{2,4},{4,6},{6,8},{8,10},{10,12},{12,14},{14,16},{16,18},{18... | collective-permute-start | bytes 712712 | tf_op jit(solution)/shard_map/ppermute | solution.py:44
  96.0 0.7 copy-start.10
  96.6 8.2 %collective-permute-start.10 = (bf16[32,3712]{1,0:T(8,128)(2,1)S(1)}, bf16[32,3712]{1,0:T(8,128)(2,1)S(1)}, u32[]{:S(2)}, u32[]{:S(2)}) collective-permute-start(bf16[32,3712]{1,0:T(8,128)(2,1)S(1)} %collective-permute-done.9), channel_id=1, source_target_pairs={{0,2},{2,4},{4,6},{6,8},{8,10},{10,12},{12,14},{14,16},{16,18},{18... | collective-permute-start | bytes 712712 | tf_op jit(solution)/shard_map/ppermute | solution.py:44
  104.9 0.7 copy-start.12
  105.6 8.2 %collective-permute-start.11 = (bf16[32,3712]{1,0:T(8,128)(2,1)S(1)}, bf16[32,3712]{1,0:T(8,128)(2,1)S(1)}, u32[]{:S(2)}, u32[]{:S(2)}) collective-permute-start(bf16[32,3712]{1,0:T(8,128)(2,1)S(1)} %collective-permute-done.10), channel_id=1, source_target_pairs={{0,2},{2,4},{4,6},{6,8},{8,10},{10,12},{12,14},{14,16},{16,18},{18... | collective-permute-start | bytes 712712 | tf_op jit(solution)/shard_map/ppermute | solution.py:44
  113.8 0.7 copy-start.13
  114.5 8.2 %collective-permute-start.12 = (bf16[32,3712]{1,0:T(8,128)(2,1)S(1)}, bf16[32,3712]{1,0:T(8,128)(2,1)S(1)}, u32[]{:S(2)}, u32[]{:S(2)}) collective-permute-start(bf16[32,3712]{1,0:T(8,128)(2,1)S(1)} %collective-permute-done.11), channel_id=1, source_target_pairs={{0,2},{2,4},{4,6},{6,8},{8,10},{10,12},{12,14},{14,16},{16,18},{18... | collective-permute-start | bytes 712712 | tf_op jit(solution)/shard_map/ppermute | solution.py:44
  122.7 0.7 copy-start.14
  123.4 8.3 %collective-permute-start.13 = (bf16[32,3712]{1,0:T(8,128)(2,1)S(1)}, bf16[32,3712]{1,0:T(8,128)(2,1)}, u32[]{:S(2)}, u32[]{:S(2)}) collective-permute-start(bf16[32,3712]{1,0:T(8,128)(2,1)S(1)} %collective-permute-done.12), channel_id=1, source_target_pairs={{0,2},{2,4},{4,6},{6,8},{8,10},{10,12},{12,14},{14,16},{16,18},{18... | collective-permute-start | bytes 712712 | tf_op jit(solution)/shard_map/ppermute | solution.py:44
  131.8 26.2 %collective-permute-start.14 = (bf16[32,3712]{1,0:T(8,128)(2,1)}, bf16[32,3712]{1,0:T(8,128)(2,1)}, u32[]{:S(2)}, u32[]{:S(2)}) collective-permute-start(bf16[32,3712]{1,0:T(8,128)(2,1)} %collective-permute-done.13), channel_id=1, source_target_pairs={{0,2},{2,4},{4,6},{6,8},{8,10},{10,12},{12,14},{14,16},{16,18},{18... | collective-permute-start | bytes 712712 | tf_op jit(solution)/shard_map/ppermute | solution.py:44
  132.7 6.9 %copy-start.6 = (bf16[32,3712]{1,0:T(8,128)(2,1)S(1)}, bf16[32,3712]{1,0:T(8,128)(2,1)}, u32[]{:S(2)}) copy-start(bf16[32,3712]{1,0:T(8,128)(2,1)} %copy-done.5) | copy-start | bytes 712708
  140.9 6.8 %copy-start.11 = (bf16[32,3712]{1,0:T(8,128)(2,1)S(1)}, bf16[32,3712]{1,0:T(8,128)(2,1)}, u32[]{:S(2)}) copy-start(bf16[32,3712]{1,0:T(8,128)(2,1)} %copy-done.10) | copy-start | bytes 712708
  214.2 0.7 copy-start.15
  214.2 1.1 copy-start.1
Sparse Core Ops, SparseCore 0:
  214.3 92.7 reduce-scatter.1
